TPU v7x, 256 devices: a whole 4x4x8 slice. The times are simulated.
256 devices in a mesh: dp: 4 (over y), section: 16 (over z, x_lo), tensor: 4 (over x_hi, core).
Axes of the slice: x: 4 (x_hi: 2, x_lo: 2; x = x_hi * 2 + x_lo), y: 4, z: 8, core: 2. Of those that a mesh axis runs over, the one named last changes fastest.
Arguments:
- saved_input: bfloat16 [16, 2, 512, 8192], P('section', None, ('dp', 'tensor')), may hold values from -6 to 6
- kv_grad: bfloat16 [16, 2, 512, 2048], P('section', None, 'dp', 'tensor'), may hold values from -1.5 to 1.5
- kv_weight: bfloat16 [16, 8192, 2048], P('section', 'dp', 'tensor'), may hold values from -0.0625 to 0.0625
- norm_gain: bfloat16 [16, 8192], P('section'), may hold values from 0.5 to 1.5
- top_grad: bfloat16 [2, 512, 8192], P(None, ('dp', 'tensor')), may hold values from -1.5 to 1.5
- noise_salt: int32 [1], replicated, may hold values from 0 to 1073741823
- step_counter: int32 [1], replicated, may hold values from 0 to 999999
Outputs:
- input_grads: bfloat16 [16, 2, 512, 8192], P('section', None, ('dp', 'tensor'))
- weight_grads: float32 [16, 8192, 2048], P('section', 'dp', 'tensor')
All inputs are finite; a program needn't handle non-finite values.
Results may differ from a plain program's by a relative error of at most 0.012.
Values may be sent and summed in bfloat16 or wider, within the bound.
No kernel may reach another device: no remote copies, remote signals or barrier semaphores. Data moves between devices by JAX's collectives and lax.ppermute only.
A program may use at most 128 MiB of HBM per device.

v0:
```python
import jax
import jax.numpy as jnp
from jax import lax
from jax.sharding import PartitionSpec as P


def mix_bits(salt, counter, layer, group, index):
    h = (
        index * jnp.int32(-1640531535)
        + salt * jnp.int32(374761393)
        + counter * jnp.int32(668265263)
    )
    h = h + layer * jnp.int32(-1028477379) + group * jnp.int32(1274126177)
    h = h ^ lax.shift_right_logical(h, jnp.int32(16))
    h = h * jnp.int32(2146121005)
    h = h ^ lax.shift_right_logical(h, jnp.int32(15))
    h = h * jnp.int32(-2073254261)
    h = h ^ lax.shift_right_logical(h, jnp.int32(16))
    return lax.shift_right_logical(h, jnp.int32(8)).astype(jnp.float32) * (1.0 / 16777216.0)


def dither(term, salt, counter, layer, group, index):
    noise = mix_bits(salt, counter, layer, group, index)
    moved = term * (1.0 + (noise - 0.5) * 0.5)
    return lax.optimization_barrier(moved.astype(jnp.bfloat16)).astype(jnp.float32)


def later_sum(branch_path):
    n_sec = lax.axis_size("section")
    m, t, d = branch_path.shape
    chunks = lax.all_to_all(
        branch_path.astype(jnp.bfloat16)[None], "section", 3, 0, tiled=True
    ).astype(jnp.float32)
    acc = jnp.zeros(chunks.shape[1:], jnp.float32)
    outs = [None] * n_sec
    for s in range(n_sec - 1, -1, -1):
        outs[s] = acc
        acc = acc + chunks[s]
    stacked = jnp.stack(outs).astype(jnp.bfloat16)
    back = lax.all_to_all(stacked, "section", 0, 3, tiled=True)
    return back[0].astype(jnp.float32)


def shards(saved_input, kv_grad, kv_weight, norm_gain, top_grad, noise_salt, step_counter):
    salt = noise_salt[0]
    counter = step_counter[0]
    layer = lax.axis_index("section")
    n_dp = lax.axis_size("dp")
    n_t = lax.axis_size("tensor")
    my_p = lax.axis_index("dp")
    my_t = lax.axis_index("tensor")
    cotan = kv_grad[0]
    weight = kv_weight[0]
    rows_p, width_t = weight.shape
    total_cols = width_t * n_t
    mb, tok_dev, d_model = saved_input.shape[1:]
    input_float = saved_input[0].astype(jnp.float32)
    inverse_scale = lax.rsqrt(jnp.mean(input_float * input_float, axis=-1, keepdims=True) + 1e-05)
    centered_input = input_float * inverse_scale
    gain_float = norm_gain[0].astype(jnp.float32)
    normed_values = (centered_input * gain_float).astype(jnp.bfloat16)
    cotan_all = lax.all_gather(cotan, "dp", axis=1, tiled=True)
    part = jnp.einsum("mtk,dk->mtd", cotan_all, weight, preferred_element_type=jnp.float32).astype(
        jnp.bfloat16
    )
    part = part.reshape(mb, n_dp * n_t, tok_dev, rows_p).transpose(1, 0, 2, 3)
    got = lax.all_to_all(part, ("dp", "tensor"), 0, 0, tiled=True)
    got = got.reshape(n_dp, n_t, mb, tok_dev, rows_p).astype(jnp.float32)
    normed_grad = got[:, 0]
    for t in range(1, n_t):
        normed_grad = normed_grad + got[:, t]
    normed_grad = normed_grad.transpose(1, 2, 0, 3).reshape(mb, tok_dev, d_model)
    hidden_gradient = normed_grad * gain_float
    branch_path = inverse_scale * (
        hidden_gradient
        - centered_input * jnp.mean(hidden_gradient * centered_input, axis=-1, keepdims=True)
    )
    later = later_sum(branch_path)
    grad_in = (top_grad.astype(jnp.float32) + branch_path + later).astype(jnp.bfloat16)
    nrm = normed_values.reshape(mb, tok_dev, n_dp, rows_p).transpose(2, 0, 1, 3)
    nrm = lax.all_to_all(nrm, "dp", 0, 0, tiled=True)
    nrm = lax.all_gather(nrm, "tensor", axis=0, tiled=False)
    cot = cotan_all.reshape(mb, n_dp, n_t, tok_dev, width_t)
    terms = jnp.einsum("tpmid,mptik->pdk", nrm, cot, preferred_element_type=jnp.float32)
    row_ids = my_p * jnp.int32(rows_p) + jnp.arange(rows_p, dtype=jnp.int32)
    index = (
        row_ids[:, None] * jnp.int32(total_cols)
        + my_t * jnp.int32(width_t)
        + jnp.arange(width_t, dtype=jnp.int32)[None, :]
    )
    wsum = jnp.zeros((rows_p, width_t), jnp.float32)
    for g in range(n_dp):
        wsum = wsum + dither(terms[g], salt, counter, layer, jnp.int32(g), index)
    return (grad_in[None], wsum[None])


def solution(mesh):
    placed = (
        P("section", None, ("dp", "tensor"), None),
        P("section", None, "dp", "tensor"),
        P("section", "dp", "tensor"),
        P("section", None),
        P(None, ("dp", "tensor"), None),
        P(),
        P(),
    )
    return jax.shard_map(
        shards,
        mesh=mesh,
        in_specs=placed,
        out_specs=(P("section", None, ("dp", "tensor"), None), P("section", "dp", "tensor")),
        check_vma=False,
    )
```

profile of v0, /device:TPU:8, one launch (start us, length us, event | category | flops | bytes accessed | tf_op | source)
XLA Modules:
  0.0 288.4 jit_solution(17948738188843804011)
XLA Ops:
  7.9 30.3 %all-gather.5.cloned.1.call-done = bf16[1,2,512,512]{3,2,1,0:T(8,128)(2,1)} async-done(((bf16[1,2,128,512]{3,2,1,0:T(8,128)(2,1)}), bf16[1,2,512,512]{3,2,1,0:T(8,128)(2,1)}) %all-gather.5.cloned.1.call-update) | async-done | bytes 1048592 | tf_op jit(solution)/shard_map/all_gather | solution.py:62
  38.2 3.6 %convolution_convert_fusion = bf16[2,512,2048]{2,1,0:T(8,128)(2,1)S(1)} fusion(bf16[1,2048,512]{2,1,0:T(8,128)(2,1)S(1)} %copy-done, bf16[1,2,512,512]{3,2,1,0:T(8,128)(2,1)} %all-gather.5.cloned.1.call-done), kind=kOutput, calls=%fused_computation.60 | convolution fusion | flops 2149580800 | bytes 7340032 | tf_op jit(solution)/shard_map/mtk,dk->mtd/dot_general | solution.py:63
  41.8 2.3 copy.237
  44.1 7.6 %all-to-all-start = ((bf16[16,2,32,2048]{3,2,1,0:T(8,128)(2,1)}), bf16[16,2,32,2048]{3,2,1,0:T(8,128)(2,1)}, u32[]{:S(2)}, u32[]{:S(2)}) async-start(bf16[16,2,32,2048]{3,2,1,0:T(8,128)(2,1)} %bitcast.145), calls=%async_computation | async-start | bytes 8388608 | tf_op jit(solution)/shard_map/all_to_all | solution.py:67
  51.9 2.7 reshape.107
  55.0 47.1 %all-to-all-done = bf16[16,2,32,2048]{3,2,1,0:T(8,128)(2,1)} async-done(((bf16[16,2,32,2048]{3,2,1,0:T(8,128)(2,1)}), bf16[16,2,32,2048]{3,2,1,0:T(8,128)(2,1)}, u32[]{:S(2)}, u32[]{:S(2)}) %all-to-all-start) | async-done | bytes 4194336 | tf_op jit(solution)/shard_map/all_to_all | solution.py:67
  102.0 3.4 %bitcast_convert_fusion = f32[4,4,2,32,2048]{4,3,2,1,0:T(8,128)S(1)} fusion(bf16[16,2,32,2048]{3,2,1,0:T(8,128)(2,1)} %all-to-all-done), kind=kLoop, calls=%fused_computation.121 | loop fusion | flops 2097152 | bytes 12582912 | tf_op jit(solution)/shard_map/convert_element_type | solution.py:68
  105.5 3.0 %multiply_reduce_fusion = (f32[2,32]{1,0:T(2,128)S(1)}, f32[4,1,2,32,2048]{4,3,2,1,0:T(8,128)S(1)}, bf16[4,2,32,2048]{3,2,1,0:T(8,128)(2,1)}) fusion(f32[2,32,4,2048]{3,2,1,0:T(4,128)S(1)} %copy-done.4, f32[2,32]{1,0:T(2,128)S(1)} %add_rsqrt_fusion, f32[4,2048]{1,0:T(4,128)S(1)} %reshape.106, f32[4,4,2,32,2048]{4,3,2,1,0:T(8,128)S(1)} %bitcast_convert_fusion), kind=kLoop, calls=%fused_computation.78 | loop fusion | flops 4718528 | bytes 13664768 | tf_op jit(solution)/shard_map/reduce_sum | solution.py:76
  108.4 5.9 %all-to-all-start.3 = ((bf16[4,2,32,2048]{3,2,1,0:T(8,128)(2,1)}), bf16[4,2,32,2048]{3,2,1,0:T(8,128)(2,1)}, u32[]{:S(2)}, u32[]{:S(2)}) async-start(bf16[4,2,32,2048]{3,2,1,0:T(8,128)(2,1)} %get-tuple-element.20), calls=%async_computation.3 | async-start | bytes 2097152 | tf_op jit(solution)/shard_map/all_to_all | solution.py:81
  114.3 2.7 copy.102
  117.0 3.6 %reshape.101 = f32[1,2,32,8192]{3,2,1,0:T(8,128)} reshape(f32[2,32,4,2048]{3,2,1,0:T(4,128)} %copy.102) | data formatting | bytes 4194304 | tf_op jit(solution)/shard_map/reshape | solution.py:72
  120.6 3.1 %multiply_convert_fusion.1 = bf16[1,2,32,8192]{3,2,1,0:T(8,128)(2,1)} fusion(f32[1,2,32,8192]{3,2,1,0:T(8,128)} %reshape.101, bf16[1,2,32,8192]{3,2,1,0:T(8,128)(2,1)S(1)} %copy-done.2, f32[2,32]{1,0:T(2,128)S(1)} %broadcast_multiply_fusion, f32[8192]{0:T(1024)S(1)} %bitcast.151, f32[2,32]{1,0:T(2,128)S(1)} %add_rsqrt_fusion), kind=kLoop, calls=%fused_computation.77 | loop fusion | flops 3670016 | bytes 4227584 | tf_op jit(solution)/shard_map/convert_element_type | solution.py:32
  123.7 9.2 %copy.105 = bf16[1,2,32,8192]{2,1,0,3:T(2,128)(2,1)} copy(bf16[1,2,32,8192]{3,2,1,0:T(8,128)(2,1)} %multiply_convert_fusion.1) | data formatting | bytes 2097152 | tf_op jit(solution)/shard_map/convert_element_type | solution.py:32
  132.8 9.9 %reshape.147 = bf16[16,2,16384]{2,1,0:T(2,128)(2,1)} reshape(bf16[8192,1,2,32]{3,2,1,0:T(2,128)(2,1)} %bitcast.143) | data formatting | bytes 2097152
  142.8 7.2 %all-to-all-start.1 = ((bf16[16,2,16384]{2,1,0:T(2,128)(2,1)}), bf16[16,2,16384]{2,1,0:T(2,128)(2,1)}, u32[]{:S(2)}, u32[]{:S(2)}) async-start(bf16[16,2,16384]{2,1,0:T(2,128)(2,1)} %reshape.147), calls=%async_computation.1 | async-start | bytes 2097152 | tf_op jit(solution)/shard_map/all_to_all | solution.py:31
  150.7 27.2 %all-to-all-done.1 = bf16[16,2,16384]{2,1,0:T(2,128)(2,1)} async-done(((bf16[16,2,16384]{2,1,0:T(2,128)(2,1)}), bf16[16,2,16384]{2,1,0:T(2,128)(2,1)}, u32[]{:S(2)}, u32[]{:S(2)}) %all-to-all-start.1) | async-done | bytes 1048608 | tf_op jit(solution)/shard_map/all_to_all | solution.py:31
  177.9 10.0 %reshape.148 = bf16[8192,1,2,32]{3,2,1,0:T(2,128)(2,1)} reshape(bf16[16,2,16384]{2,1,0:T(2,128)(2,1)} %all-to-all-done.1) | data formatting | bytes 2097152
  187.9 9.0 %copy.106 = bf16[1,2,32,8192]{3,2,1,0:T(8,128)(2,1)} copy(bf16[1,2,32,8192]{2,1,0,3:T(2,128)(2,1)} %bitcast.144) | data formatting | bytes 2097152 | tf_op jit(solution)/shard_map/all_to_all | solution.py:31
  196.9 1.6 copy.154
  198.6 1.8 fusion.61
  211.0 7.5 %stack.3 = bf16[16,2,32,512]{3,0,2,1:T(8,128)(2,1)} concatenate(bf16[1,2,32,512]{3,0,2,1:T(2,128)(2,1)S(1)} %fusion.53, bf16[1,2,32,512]{3,0,2,1:T(2,128)(2,1)S(1)} %copy.122, bf16[1,2,32,512]{3,0,2,1:T(2,128)(2,1)} %copy.123, bf16[1,2,32,512]{3,0,2,1:T(2,128)(2,1)S(1)} %copy.124, bf16[1,2,32,512]{3,0,2,1:T(2,128)(2,1)} %copy.125, bf16[1,2,32,512]{3,0,2,1:T(2,128)(2,1)} %copy.126, ...), dimensions={0} | concatenate | bytes 2097152 | tf_op jit(solution)/shard_map/stack | solution.py:39
  218.5 2.8 copy.135
  221.3 4.6 %all-to-all-start.2 = ((bf16[16,2,32,512]{3,2,1,0:T(8,128)(2,1)}), bf16[16,2,32,512]{3,2,1,0:T(8,128)(2,1)}, u32[]{:S(2)}, u32[]{:S(2)}) async-start(bf16[16,2,32,512]{3,2,1,0:T(8,128)(2,1)} %copy.135), calls=%async_computation.2 | async-start | bytes 2097152 | tf_op jit(solution)/shard_map/all_to_all | solution.py:40
  227.2 1.6 copy.153
  228.7 23.9 %all-to-all-done.2 = bf16[16,2,32,512]{3,2,1,0:T(8,128)(2,1)} async-done(((bf16[16,2,32,512]{3,2,1,0:T(8,128)(2,1)}), bf16[16,2,32,512]{3,2,1,0:T(8,128)(2,1)}, u32[]{:S(2)}, u32[]{:S(2)}) %all-to-all-start.2) | async-done | bytes 1048608 | tf_op jit(solution)/shard_map/all_to_all | solution.py:40
  252.6 1.5 convert_bitcast_fusion
  254.1 2.5 copy.136
  256.7 2.9 %reshape.110 = f32[2,32,8192]{2,1,0:T(8,128)} reshape(f32[1,2,32,16,512]{4,3,2,1,0:T(8,128)} %copy.136) | data formatting | bytes 4194304 | tf_op jit(solution)/shard_map/convert_element_type | solution.py:41
  259.6 3.5 %fusion.49 = bf16[1,2,32,8192]{3,2,1,0:T(8,128)(2,1)} fusion(f32[2,32,8192]{2,1,0:T(8,128)} %reshape.110, bf16[1,2,32,8192]{3,2,1,0:T(8,128)(2,1)S(1)} %copy-done.2, f32[2,32,8192]{2,1,0:T(8,128)S(1)} %bitcast.146, bf16[2,32,8192]{2,1,0:T(8,128)(2,1)} %param.11, f32[2,32]{1,0:T(2,128)S(1)} %broadcast_multiply_fusion, f32[8192]{0:T(1024)S(1)} %bitcast.152, ...), kind=kLoop, calls=%fused_computation.80 | loop fusion | flops 5242880 | bytes 7373312 | tf_op jit(solution)/shard_map/broadcast_in_dim | solution.py:94
  263.1 4.9 %convolution_bitcast_fusion = f32[4,2048,512]{2,1,0:T(8,128)S(1)} fusion(bf16[4,4,2,32,2048]{4,3,2,1,0:T(8,128)(2,1)} %bitcast.154, bf16[2,4,4,32,512]{4,3,2,1,0:T(8,128)(2,1)} %bitcast.155), kind=kOutput, calls=%fused_computation | convolution fusion | flops 2147483648 | bytes 22020096 | tf_op jit(solution)/shard_map/tpmid,mptik->pdk/dot_general | solution.py:84
  268.0 10.4 %fusion.39 = (bf16[2048,512]{1,0:T(8,128)(2,1)S(1)}, bf16[2048,512]{1,0:T(8,128)(2,1)S(1)}, bf16[2048,512]{1,0:T(8,128)(2,1)S(1)}, bf16[2048,512]{1,0:T(8,128)(2,1)S(1)}) fusion(f32[4,2048,512]{2,1,0:T(8,128)S(1)} %convolution_bitcast_fusion, s32[]{:T(128)S(6)} %mul.216, s32[]{:T(128)} %bitcast.37, s32[]{:T(128)} %bitcast.36, s32[2048]{0:T(1024)S(1)} %multiply_add_fusion), kind=kLoop, calls=%fused_computation.59 | loop fusion | flops 75497472 | bytes 25174028 | tf_op jit(solution)/shard_map/convert_element_type | solution.py:25
  278.4 3.2 %add_bitcast_fusion = f32[1,2048,512]{2,1,0:T(8,128)} fusion(bf16[2048,512]{1,0:T(8,128)(2,1)S(1)} %get-tuple-element.17, bf16[2048,512]{1,0:T(8,128)(2,1)S(1)} %get-tuple-element.18, bf16[2048,512]{1,0:T(8,128)(2,1)S(1)} %get-tuple-element.19, bf16[2048,512]{1,0:T(8,128)(2,1)S(1)} %get-tuple-element.16), kind=kLoop, calls=%fused_computation.54 | loop fusion | flops 7340032 | bytes 12582912 | tf_op jit(solution)/shard_map/broadcast_in_dim | solution.py:94
  (53 shorter events, 12.5 us)
Async XLA Ops:
  7.2 31.0 %copy-start = (bf16[1,2048,512]{2,1,0:T(8,128)(2,1)S(1)}, bf16[1,2048,512]{2,1,0:T(8,128)(2,1)}, u32[]{:S(2)}) copy-start(bf16[1,2048,512]{2,1,0:T(8,128)(2,1)} %param.9) | copy-start | bytes 6291460
  7.2 31.0 %all-gather.5.cloned.1.call-start = ((), (), s32[]{:S(2)}) async-start(), calls=%async_computation.4 | async-start | bytes 1310720 | tf_op jit(solution)/shard_map/all_gather | solution.py:62
  44.1 7.6 %copy-start.7 = (bf16[1,8192]{1,0:T(2,128)(2,1)S(1)}, bf16[1,8192]{1,0:T(2,128)(2,1)}, u32[]{:S(2)}) copy-start(bf16[1,8192]{1,0:T(2,128)(2,1)} %param.10) | copy-start | bytes 49156
  44.1 7.8 %copy-start.2 = (bf16[1,2,32,8192]{3,2,1,0:T(8,128)(2,1)S(1)}, bf16[1,2,32,8192]{3,2,1,0:T(8,128)(2,1)}, u32[]{:S(2)}) copy-start(bf16[1,2,32,8192]{3,2,1,0:T(8,128)(2,1)} %param.7) | copy-start | bytes 3145732
  44.1 57.9 %all-to-all-start = ((bf16[16,2,32,2048]{3,2,1,0:T(8,128)(2,1)}), bf16[16,2,32,2048]{3,2,1,0:T(8,128)(2,1)}, u32[]{:S(2)}, u32[]{:S(2)}) async-start(bf16[16,2,32,2048]{3,2,1,0:T(8,128)(2,1)} %bitcast.145), calls=%async_computation | async-start | bytes 8388608 | tf_op jit(solution)/shard_map/all_to_all | solution.py:67
  51.8 68.8 %copy-start.5 = (f32[1,8192]{1,0:T(1,128)}, f32[1,8192]{1,0:T(1,128)S(1)}, u32[]{:S(2)}) copy-start(f32[1,8192]{1,0:T(1,128)S(1)} %convert_element_type.151) | copy-start | bytes 98308
  102.0 3.4 %copy-start.4 = (f32[2,32,4,2048]{3,2,1,0:T(4,128)S(1)}, f32[2,32,4,2048]{3,2,1,0:T(4,128)}, u32[]{:S(2)}) copy-start(f32[2,32,4,2048]{3,2,1,0:T(4,128)} %reshape.107) | copy-start | bytes 6291460
  108.4 34.3 %all-to-all-start.3 = ((bf16[4,2,32,2048]{3,2,1,0:T(8,128)(2,1)}), bf16[4,2,32,2048]{3,2,1,0:T(8,128)(2,1)}, u32[]{:S(2)}, u32[]{:S(2)}) async-start(bf16[4,2,32,2048]{3,2,1,0:T(8,128)(2,1)} %get-tuple-element.20), calls=%async_computation.3 | async-start | bytes 2097152 | tf_op jit(solution)/shard_map/all_to_all | solution.py:81
  142.8 35.1 %all-to-all-start.1 = ((bf16[16,2,16384]{2,1,0:T(2,128)(2,1)}), bf16[16,2,16384]{2,1,0:T(2,128)(2,1)}, u32[]{:S(2)}, u32[]{:S(2)}) async-start(bf16[16,2,16384]{2,1,0:T(2,128)(2,1)} %reshape.147), calls=%async_computation.1 | async-start | bytes 2097152 | tf_op jit(solution)/shard_map/all_to_all | solution.py:31
  150.0 113.2 %all-gather.7.cloned.1.call-start = ((), (), s32[]{:S(2)}) async-start(), calls=%async_computation.5 | async-start | bytes 5242880 | tf_op jit(solution)/shard_map/all_gather | solution.py:82
  221.3 31.3 %all-to-all-start.2 = ((bf16[16,2,32,512]{3,2,1,0:T(8,128)(2,1)}), bf16[16,2,32,512]{3,2,1,0:T(8,128)(2,1)}, u32[]{:S(2)}, u32[]{:S(2)}) async-start(bf16[16,2,32,512]{3,2,1,0:T(8,128)(2,1)} %copy.135), calls=%async_computation.2 | async-start | bytes 2097152 | tf_op jit(solution)/shard_map/all_to_all | solution.py:40
  254.1 5.5 %copy-start.6 = (f32[1,8192]{1,0:T(1,128)S(1)}, f32[1,8192]{1,0:T(1,128)}, u32[]{:S(2)}) copy-start(f32[1,8192]{1,0:T(1,128)} %copy-done.5) | copy-start | bytes 98308
  256.7 2.9 %copy-start.3 = (f32[4,2,4,8,2048]{4,3,0,2,1:T(8,128)S(1)}, f32[4,2,4,8,2048]{4,3,0,2,1:T(8,128)}, u32[]{:S(2)}) copy-start(f32[4,2,4,8,2048]{4,3,0,2,1:T(8,128)} %copy.153) | copy-start | bytes 6291460
  278.4 3.2 %copy-start.1 = (bf16[1,2048,512]{2,1,0:T(8,128)(2,1)S(1)}, bf16[1,2048,512]{2,1,0:T(8,128)(2,1)}, u32[]{:S(2)}) copy-start(bf16[1,2048,512]{2,1,0:T(8,128)(2,1)} %param.9) | copy-start | bytes 6291460
Sparse Core Ops, SparseCore 0:
  9.8 28.3 all-gather.4
  152.6 46.6 all-gather.6
where the time goes:
time: 290 us; the launch traced here: 288 us
  waiting for transfers between devices  130 us (45%)
  local copies, waits for them, and re-layouts  80.4 us (28%)
  other arithmetic  28.9 us (10%)
  starting transfers between devices  25.5 us (9%)
  between operations  15.6 us (5%)
  matrix products  8.46 us (3%)
    all_to_all x1, waiting for transfers between devices, shards(): got = lax.all_to_all(part, ('dp', 'tensor'), 0, 0, tiled=True)  47.1 us
    all_gather x1, waiting for transfers between devices, shards(): cotan_all = lax.all_gather(cotan, 'dp', axis=1, tiled=True)  30.3 us
    all_to_all x1, waiting for transfers between devices, later_sum(): lax.all_to_all(branch_path.astype(jnp.bfloat16)[None], 'section', 3, 0, t...  27.2 us
    all_to_all x1, waiting for transfers between devices, later_sum(): back = lax.all_to_all(stacked, 'section', 0, 3, tiled=True)  23.9 us
    unnamed x20, local copies, waits for them, and re-layouts  21.6 us
    another operation x3, local copies, waits for them, and re-layouts, later_sum(): stacked = jnp.stack(outs).astype(jnp.bfloat16)  11 us
    convert_element_type x1, other arithmetic, dither(): moved.astype(jnp.bfloat16)  10.4 us
    another operation x14, local copies, waits for them, and re-layouts  9.33 us
  transfers between devices with their start and end apart: 6, of which 4 were waited for; matrix products, arithmetic and copies ran while one was open for 30% of the time, Pallas kernels for 0%

commit v1 on v0

--- a/solution.py
+++ b/solution.py
@@ -59,7 +59,9 @@
     centered_input = input_float * inverse_scale
     gain_float = norm_gain[0].astype(jnp.float32)
     normed_values = (centered_input * gain_float).astype(jnp.bfloat16)
-    cotan_all = lax.all_gather(cotan, "dp", axis=1, tiled=True)
+    cotan_all = jnp.concatenate(
+        lax.all_to_all(jnp.stack([cotan] * lax.axis_size("dp")), "dp", 0, 0), axis=1
+    )
     part = jnp.einsum("mtk,dk->mtd", cotan_all, weight, preferred_element_type=jnp.float32).astype(
         jnp.bfloat16
     )

time: 290 us -> 279 us (0.962)
  waiting for transfers between devices: 130 us -> 98.8 us
  blocking collectives: 0 us -> 18.3 us
    all_gather x1 -> x0, waiting for transfers between devices: 30.3 us -> none  [shards(): cotan_all = lax.all_gather(cotan, 'dp', axis=1, tiled=True)]
    all_to_all x0 -> x1, blocking collectives: none -> 18.3 us  [shards(): lax.all_to_all(jnp.stack([cotan] * lax.axis_size('dp')), 'dp', 0, 0)]
    another operation x14 -> x15, local copies, waits for them, and re-layouts: 9.33 us -> 10.5 us
    unnamed x20 -> x22, local copies, waits for them, and re-layouts: 21.6 us -> 22.6 us
  transfers between devices with their start and end apart: 6 -> 5, of which waited for: 4 -> 3; matrix products, arithmetic and copies ran while one was open for 30% -> 31% of each run, Pallas kernels for 0% -> 0%
where the time goes in v1:
time: 279 us; the launch traced here: 277 us
  waiting for transfers between devices  98.8 us (35%)
  local copies, waits for them, and re-layouts  82.5 us (30%)
  other arithmetic  28.9 us (10%)
  starting transfers between devices  26 us (9%)
  blocking collectives  18.3 us (7%)
  between operations  15.6 us (6%)
  matrix products  7.26 us (3%)
    all_to_all x1, waiting for transfers between devices, shards(): got = lax.all_to_all(part, ('dp', 'tensor'), 0, 0, tiled=True)  47.1 us
    all_to_all x1, waiting for transfers between devices, later_sum(): lax.all_to_all(branch_path.astype(jnp.bfloat16)[None], 'section', 3, 0, t...  27.2 us
    all_to_all x1, waiting for transfers between devices, later_sum(): back = lax.all_to_all(stacked, 'section', 0, 3, tiled=True)  23.8 us
    unnamed x22, local copies, waits for them, and re-layouts  22.6 us
    all_to_all x1, blocking collectives, shards(): lax.all_to_all(jnp.stack([cotan] * lax.axis_size('dp')), 'dp', 0, 0)  18.3 us
    another operation x3, local copies, waits for them, and re-layouts, later_sum(): stacked = jnp.stack(outs).astype(jnp.bfloat16)  11 us
    convert_element_type x1, other arithmetic, dither(): moved.astype(jnp.bfloat16)  10.4 us
    another operation x14, local copies, waits for them, and re-layouts  9.27 us
  transfers between devices with their start and end apart: 5, of which 3 were waited for; matrix products, arithmetic and copies ran while one was open for 31% of the time, Pallas kernels for 0%

profile of v1, /device:TPU:8, one launch (start us, length us, event | category | flops | bytes accessed | tf_op | source)
XLA Modules:
  0.0 277.3 jit_solution(15659947959631619552)
XLA Ops:
  8.4 18.3 %all_to_all.33 = bf16[4,2,128,512]{3,2,1,0:T(8,128)(2,1)S(1)} all-to-all(bf16[4,2,128,512]{3,2,1,0:T(8,128)(2,1)S(1)} %stack.5), channel_id=1, replica_groups=mesh['dp'=4,'section'=16,'tensor'=4] {'dp'}, dimensions={0} | all-to-all | bytes 2097152 | tf_op jit(solution)/shard_map/all_to_all | solution.py:63
  27.8 2.4 convolution_convert_fusion
  30.2 2.3 copy.272
  32.5 6.5 %all-to-all-start.1 = ((bf16[16,2,32,2048]{3,2,1,0:T(8,128)(2,1)}), bf16[16,2,32,2048]{3,2,1,0:T(8,128)(2,1)}, u32[]{:S(2)}, u32[]{:S(2)}) async-start(bf16[16,2,32,2048]{3,2,1,0:T(8,128)(2,1)} %bitcast.148), calls=%async_computation.1 | async-start | bytes 8388608 | tf_op jit(solution)/shard_map/all_to_all | solution.py:69
  39.2 2.7 reshape.112
  42.2 47.1 %all-to-all-done.1 = bf16[16,2,32,2048]{3,2,1,0:T(8,128)(2,1)} async-done(((bf16[16,2,32,2048]{3,2,1,0:T(8,128)(2,1)}), bf16[16,2,32,2048]{3,2,1,0:T(8,128)(2,1)}, u32[]{:S(2)}, u32[]{:S(2)}) %all-to-all-start.1) | async-done | bytes 4194336 | tf_op jit(solution)/shard_map/all_to_all | solution.py:69
  89.3 3.4 %bitcast_convert_fusion = f32[4,4,2,32,2048]{4,3,2,1,0:T(8,128)S(1)} fusion(bf16[16,2,32,2048]{3,2,1,0:T(8,128)(2,1)} %all-to-all-done.1), kind=kLoop, calls=%fused_computation.120 | loop fusion | flops 2097152 | bytes 12582912 | tf_op jit(solution)/shard_map/convert_element_type | solution.py:70
  92.7 3.0 %multiply_reduce_fusion = (f32[2,32]{1,0:T(2,128)S(1)}, f32[4,1,2,32,2048]{4,3,2,1,0:T(8,128)S(1)}, bf16[4,2,32,2048]{3,2,1,0:T(8,128)(2,1)}) fusion(f32[2,32,4,2048]{3,2,1,0:T(4,128)S(1)} %copy-done.4, f32[2,32]{1,0:T(2,128)S(1)} %add_rsqrt_fusion, f32[4,2048]{1,0:T(4,128)S(1)} %reshape.111, f32[4,4,2,32,2048]{4,3,2,1,0:T(8,128)S(1)} %bitcast_convert_fusion), kind=kLoop, calls=%fused_computation.78 | loop fusion | flops 4718528 | bytes 13664768 | tf_op jit(solution)/shard_map/reduce_sum | solution.py:78
  95.7 5.9 %all-to-all-start.4 = ((bf16[4,2,32,2048]{3,2,1,0:T(8,128)(2,1)}), bf16[4,2,32,2048]{3,2,1,0:T(8,128)(2,1)}, u32[]{:S(2)}, u32[]{:S(2)}) async-start(bf16[4,2,32,2048]{3,2,1,0:T(8,128)(2,1)} %get-tuple-element.20), calls=%async_computation.4 | async-start | bytes 2097152 | tf_op jit(solution)/shard_map/all_to_all | solution.py:83
  101.6 2.7 copy.136
  104.2 3.7 %reshape.107 = f32[1,2,32,8192]{3,2,1,0:T(8,128)} reshape(f32[2,32,4,2048]{3,2,1,0:T(4,128)} %copy.136) | data formatting | bytes 4194304 | tf_op jit(solution)/shard_map/reshape | solution.py:74
  107.9 3.1 %multiply_convert_fusion.1 = bf16[1,2,32,8192]{3,2,1,0:T(8,128)(2,1)} fusion(f32[1,2,32,8192]{3,2,1,0:T(8,128)} %reshape.107, bf16[1,2,32,8192]{3,2,1,0:T(8,128)(2,1)S(1)} %copy-done.2, f32[2,32]{1,0:T(2,128)S(1)} %broadcast_multiply_fusion, f32[8192]{0:T(1024)S(1)} %bitcast.156, f32[2,32]{1,0:T(2,128)S(1)} %add_rsqrt_fusion), kind=kLoop, calls=%fused_computation.77 | loop fusion | flops 3670016 | bytes 4227584 | tf_op jit(solution)/shard_map/convert_element_type | solution.py:32
  111.0 9.2 %copy.139 = bf16[1,2,32,8192]{2,1,0,3:T(2,128)(2,1)} copy(bf16[1,2,32,8192]{3,2,1,0:T(8,128)(2,1)} %multiply_convert_fusion.1) | data formatting | bytes 2097152 | tf_op jit(solution)/shard_map/convert_element_type | solution.py:32
  120.1 9.9 %reshape.150 = bf16[16,2,16384]{2,1,0:T(2,128)(2,1)} reshape(bf16[8192,1,2,32]{3,2,1,0:T(2,128)(2,1)} %bitcast.146) | data formatting | bytes 2097152
  130.0 9.0 %all-to-all-start.2 = ((bf16[16,2,16384]{2,1,0:T(2,128)(2,1)}), bf16[16,2,16384]{2,1,0:T(2,128)(2,1)}, u32[]{:S(2)}, u32[]{:S(2)}) async-start(bf16[16,2,16384]{2,1,0:T(2,128)(2,1)} %reshape.150), calls=%async_computation.2 | async-start | bytes 2097152 | tf_op jit(solution)/shard_map/all_to_all | solution.py:31
  139.8 27.2 %all-to-all-done.2 = bf16[16,2,16384]{2,1,0:T(2,128)(2,1)} async-done(((bf16[16,2,16384]{2,1,0:T(2,128)(2,1)}), bf16[16,2,16384]{2,1,0:T(2,128)(2,1)}, u32[]{:S(2)}, u32[]{:S(2)}) %all-to-all-start.2) | async-done | bytes 1048608 | tf_op jit(solution)/shard_map/all_to_all | solution.py:31
  167.0 10.0 %reshape.151 = bf16[8192,1,2,32]{3,2,1,0:T(2,128)(2,1)} reshape(bf16[16,2,16384]{2,1,0:T(2,128)(2,1)} %all-to-all-done.2) | data formatting | bytes 2097152
  177.0 9.0 %copy.140 = bf16[1,2,32,8192]{3,2,1,0:T(8,128)(2,1)} copy(bf16[1,2,32,8192]{2,1,0,3:T(2,128)(2,1)} %bitcast.147) | data formatting | bytes 2097152 | tf_op jit(solution)/shard_map/all_to_all | solution.py:31
  186.0 1.6 copy.189
  187.7 1.8 fusion.60
  199.9 7.5 %stack.6 = bf16[16,2,32,512]{3,0,2,1:T(8,128)(2,1)} concatenate(bf16[1,2,32,512]{3,0,2,1:T(2,128)(2,1)S(1)} %fusion.52, bf16[1,2,32,512]{3,0,2,1:T(2,128)(2,1)S(1)} %copy.156, bf16[1,2,32,512]{3,0,2,1:T(2,128)(2,1)} %copy.157, bf16[1,2,32,512]{3,0,2,1:T(2,128)(2,1)S(1)} %copy.158, bf16[1,2,32,512]{3,0,2,1:T(2,128)(2,1)} %copy.159, bf16[1,2,32,512]{3,0,2,1:T(2,128)(2,1)} %copy.160, ...), dimensions={0} | concatenate | bytes 2097152 | tf_op jit(solution)/shard_map/stack | solution.py:39
  207.4 2.8 copy.169
  210.2 4.6 %all-to-all-start.3 = ((bf16[16,2,32,512]{3,2,1,0:T(8,128)(2,1)}), bf16[16,2,32,512]{3,2,1,0:T(8,128)(2,1)}, u32[]{:S(2)}, u32[]{:S(2)}) async-start(bf16[16,2,32,512]{3,2,1,0:T(8,128)(2,1)} %copy.169), calls=%async_computation.3 | async-start | bytes 2097152 | tf_op jit(solution)/shard_map/all_to_all | solution.py:40
  216.1 1.6 copy.188
  217.7 23.8 %all-to-all-done.3 = bf16[16,2,32,512]{3,2,1,0:T(8,128)(2,1)} async-done(((bf16[16,2,32,512]{3,2,1,0:T(8,128)(2,1)}), bf16[16,2,32,512]{3,2,1,0:T(8,128)(2,1)}, u32[]{:S(2)}, u32[]{:S(2)}) %all-to-all-start.3) | async-done | bytes 1048608 | tf_op jit(solution)/shard_map/all_to_all | solution.py:40
  241.5 1.5 convert_bitcast_fusion
  243.0 2.5 copy.170
  245.6 2.9 %reshape.115 = f32[2,32,8192]{2,1,0:T(8,128)} reshape(f32[1,2,32,16,512]{4,3,2,1,0:T(8,128)} %copy.170) | data formatting | bytes 4194304 | tf_op jit(solution)/shard_map/convert_element_type | solution.py:41
  248.5 3.5 %fusion.49 = bf16[1,2,32,8192]{3,2,1,0:T(8,128)(2,1)} fusion(f32[2,32,8192]{2,1,0:T(8,128)} %reshape.115, bf16[1,2,32,8192]{3,2,1,0:T(8,128)(2,1)S(1)} %copy-done.2, f32[2,32,8192]{2,1,0:T(8,128)S(1)} %bitcast.149, bf16[2,32,8192]{2,1,0:T(8,128)(2,1)} %param.11, f32[2,32]{1,0:T(2,128)S(1)} %broadcast_multiply_fusion, f32[8192]{0:T(1024)S(1)} %bitcast.157, ...), kind=kLoop, calls=%fused_computation.80 | loop fusion | flops 5242880 | bytes 7373312 | tf_op jit(solution)/shard_map/broadcast_in_dim | solution.py:96
  252.0 4.9 %convolution_bitcast_fusion = f32[4,2048,512]{2,1,0:T(8,128)S(1)} fusion(bf16[4,4,2,32,2048]{4,3,2,1,0:T(8,128)(2,1)} %bitcast.160, bf16[2,4,4,32,512]{4,3,2,0,1:T(8,128)(2,1)} %bitcast.154), kind=kOutput, calls=%fused_computation | convolution fusion | flops 2147483648 | bytes 22020096 | tf_op jit(solution)/shard_map/tpmid,mptik->pdk/dot_general | solution.py:86
  256.9 10.4 %fusion.39 = (bf16[2048,512]{1,0:T(8,128)(2,1)S(1)}, bf16[2048,512]{1,0:T(8,128)(2,1)S(1)}, bf16[2048,512]{1,0:T(8,128)(2,1)S(1)}, bf16[2048,512]{1,0:T(8,128)(2,1)S(1)}) fusion(f32[4,2048,512]{2,1,0:T(8,128)S(1)} %convolution_bitcast_fusion, s32[]{:T(128)S(6)} %mul.216, s32[]{:T(128)} %bitcast.40, s32[]{:T(128)} %bitcast.39, s32[2048]{0:T(1024)S(1)} %multiply_add_fusion), kind=kLoop, calls=%fused_computation.59 | loop fusion | flops 75497472 | bytes 25174028 | tf_op jit(solution)/shard_map/convert_element_type | solution.py:25
  267.3 3.2 %add_bitcast_fusion = f32[1,2048,512]{2,1,0:T(8,128)} fusion(bf16[2048,512]{1,0:T(8,128)(2,1)S(1)} %get-tuple-element.17, bf16[2048,512]{1,0:T(8,128)(2,1)S(1)} %get-tuple-element.18, bf16[2048,512]{1,0:T(8,128)(2,1)S(1)} %get-tuple-element.19, bf16[2048,512]{1,0:T(8,128)(2,1)S(1)} %get-tuple-element.16), kind=kLoop, calls=%fused_computation.54 | loop fusion | flops 7340032 | bytes 12582912 | tf_op jit(solution)/shard_map/broadcast_in_dim | solution.py:96
  (55 shorter events, 13.9 us)
Async XLA Ops:
  7.2 20.6 %copy-start = (bf16[1,2048,512]{2,1,0:T(8,128)(2,1)S(1)}, bf16[1,2048,512]{2,1,0:T(8,128)(2,1)}, u32[]{:S(2)}) copy-start(bf16[1,2048,512]{2,1,0:T(8,128)(2,1)} %param.9) | copy-start | bytes 6291460
  26.7 1.1 copy-start.5
  32.5 6.5 %copy-start.8 = (bf16[1,8192]{1,0:T(2,128)(2,1)S(1)}, bf16[1,8192]{1,0:T(2,128)(2,1)}, u32[]{:S(2)}) copy-start(bf16[1,8192]{1,0:T(2,128)(2,1)} %param.10) | copy-start | bytes 49156
  32.5 6.7 %copy-start.2 = (bf16[1,2,32,8192]{3,2,1,0:T(8,128)(2,1)S(1)}, bf16[1,2,32,8192]{3,2,1,0:T(8,128)(2,1)}, u32[]{:S(2)}) copy-start(bf16[1,2,32,8192]{3,2,1,0:T(8,128)(2,1)} %param.7) | copy-start | bytes 3145732
  32.5 56.8 %all-to-all-start.1 = ((bf16[16,2,32,2048]{3,2,1,0:T(8,128)(2,1)}), bf16[16,2,32,2048]{3,2,1,0:T(8,128)(2,1)}, u32[]{:S(2)}, u32[]{:S(2)}) async-start(bf16[16,2,32,2048]{3,2,1,0:T(8,128)(2,1)} %bitcast.148), calls=%async_computation.1 | async-start | bytes 8388608 | tf_op jit(solution)/shard_map/all_to_all | solution.py:69
  39.1 68.8 %copy-start.6 = (f32[1,8192]{1,0:T(1,128)}, f32[1,8192]{1,0:T(1,128)S(1)}, u32[]{:S(2)}) copy-start(f32[1,8192]{1,0:T(1,128)S(1)} %convert_element_type.151) | copy-start | bytes 98308
  89.3 3.4 %copy-start.4 = (f32[2,32,4,2048]{3,2,1,0:T(4,128)S(1)}, f32[2,32,4,2048]{3,2,1,0:T(4,128)}, u32[]{:S(2)}) copy-start(f32[2,32,4,2048]{3,2,1,0:T(4,128)} %reshape.112) | copy-start | bytes 6291460
  95.7 34.4 %all-to-all-start.4 = ((bf16[4,2,32,2048]{3,2,1,0:T(8,128)(2,1)}), bf16[4,2,32,2048]{3,2,1,0:T(8,128)(2,1)}, u32[]{:S(2)}, u32[]{:S(2)}) async-start(bf16[4,2,32,2048]{3,2,1,0:T(8,128)(2,1)} %get-tuple-element.20), calls=%async_computation.4 | async-start | bytes 2097152 | tf_op jit(solution)/shard_map/all_to_all | solution.py:83
  130.0 37.0 %all-to-all-start.2 = ((bf16[16,2,16384]{2,1,0:T(2,128)(2,1)}), bf16[16,2,16384]{2,1,0:T(2,128)(2,1)}, u32[]{:S(2)}, u32[]{:S(2)}) async-start(bf16[16,2,16384]{2,1,0:T(2,128)(2,1)} %reshape.150), calls=%async_computation.2 | async-start | bytes 2097152 | tf_op jit(solution)/shard_map/all_to_all | solution.py:31
  139.0 113.0 %all-gather.3.cloned.1.call-start = ((), (), s32[]{:S(2)}) async-start(), calls=%async_computation.5 | async-start | bytes 5242880 | tf_op jit(solution)/shard_map/all_gather | solution.py:84
  210.2 31.3 %all-to-all-start.3 = ((bf16[16,2,32,512]{3,2,1,0:T(8,128)(2,1)}), bf16[16,2,32,512]{3,2,1,0:T(8,128)(2,1)}, u32[]{:S(2)}, u32[]{:S(2)}) async-start(bf16[16,2,32,512]{3,2,1,0:T(8,128)(2,1)} %copy.169), calls=%async_computation.3 | async-start | bytes 2097152 | tf_op jit(solution)/shard_map/all_to_all | solution.py:40
  243.0 5.5 %copy-start.7 = (f32[1,8192]{1,0:T(1,128)S(1)}, f32[1,8192]{1,0:T(1,128)}, u32[]{:S(2)}) copy-start(f32[1,8192]{1,0:T(1,128)} %copy-done.6) | copy-start | bytes 98308
  245.6 2.9 %copy-start.3 = (f32[4,2,4,8,2048]{4,3,0,2,1:T(8,128)S(1)}, f32[4,2,4,8,2048]{4,3,0,2,1:T(8,128)}, u32[]{:S(2)}) copy-start(f32[4,2,4,8,2048]{4,3,0,2,1:T(8,128)} %copy.188) | copy-start | bytes 6291460
  267.3 3.2 %copy-start.1 = (bf16[1,2048,512]{2,1,0:T(8,128)(2,1)S(1)}, bf16[1,2048,512]{2,1,0:T(8,128)(2,1)}, u32[]{:S(2)}) copy-start(bf16[1,2048,512]{2,1,0:T(8,128)(2,1)} %param.9) | copy-start | bytes 6291460
Sparse Core Ops, SparseCore 0:
  141.7 46.6 all-gather.2
